TPU v7x, 32 devices: a whole 2x2x4 slice. The times are simulated.
32 devices in a mesh: dp: 4 (over z), expert: 8 (over y, x, core).
Axes of the slice: x: 2, y: 2, z: 4, core: 2. Of those that a mesh axis runs over, the one named last changes fastest.
Arguments:
- tokens: bfloat16 [384, 4096], P('expert', 'dp'), may hold values from -6 to 6
- out_grad: bfloat16 [384, 4096], P('expert', 'dp'), may hold values from -6 to 6
- expert_ids: int32 [384, 8], P('expert'), may hold values from 0 to 63, all different within a row; in each aligned block of 48 rows (0 to 47, 48 to 95, ...) at most 12 rows name the same one
- route_weights: float32 [384, 8], P('expert'), may hold values from 0.05 to 1
- gate_weight: bfloat16 [64, 4096, 768], P('expert', 'dp'), may hold values from -0.09375 to 0.09375
- up_weight: bfloat16 [64, 4096, 768], P('expert', 'dp'), may hold values from -0.09375 to 0.09375
- down_weight: bfloat16 [64, 768, 4096], P('expert', None, 'dp'), may hold values from -0.21875 to 0.21875
Outputs:
- layer_out: bfloat16 [384, 4096], P('expert', 'dp')
- grad_tokens: bfloat16 [384, 4096], P('expert', 'dp')
- gate_grad: bfloat16 [64, 4096, 768], P('expert', 'dp')
- up_grad: bfloat16 [64, 4096, 768], P('expert', 'dp')
- down_grad: bfloat16 [64, 768, 4096], P('expert', None, 'dp')
Inputs may be any that keep to these rules, and one draw needn't show every extreme that they name: `expert_ids`: each row names 8 different experts. In the 48 rows of one index of the expert axis no expert is named more than 12 times, and in every draw some expert is named exactly 12 times there.
All inputs are finite; a program needn't handle non-finite values.
Results may differ from a plain program's by a relative error of at most 0.029.
Values may be sent and summed in bfloat16 or wider, within the bound.
No kernel may reach another device: no remote copies, remote signals or barrier semaphores. Data moves between devices by JAX's collectives and lax.ppermute only.
A program may use at most 128 MiB of HBM per device.

v0:
```python
import jax
import jax.numpy as jnp
from jax import lax
from jax.sharding import PartitionSpec as P


def swiglu_parts(gate_sum, up_sum, back_sum):
    logistic = jax.nn.sigmoid(gate_sum)
    activated = gate_sum * logistic
    hidden = (activated * up_sum).astype(jnp.bfloat16)
    gate_delta = (back_sum * up_sum * logistic * (1.0 + gate_sum * (1.0 - logistic))).astype(
        jnp.bfloat16
    )
    up_delta = (back_sum * activated).astype(jnp.bfloat16)
    return (hidden, gate_delta, up_delta)


def local(tokens, out_grad, expert_ids, route_weights, gate_weight, up_weight, down_weight):
    token_count, width_dev = tokens.shape
    per_token = expert_ids.shape[1]
    local_experts = gate_weight.shape[0]
    hidden_units = gate_weight.shape[2]
    sources = lax.axis_size("expert")
    experts = local_experts * sources
    capacity = 2 * token_count * per_token // experts
    slot_count = token_count * per_token
    flat_ids = expert_ids.reshape(slot_count)
    position = jnp.arange(slot_count, dtype=jnp.int32)
    earlier = (flat_ids[None, :] == flat_ids[:, None]) & (position[None, :] < position[:, None])
    slot_rank = jnp.sum(earlier.astype(jnp.int32), axis=1)
    slot_place = (flat_ids * capacity + slot_rank).reshape(token_count, per_token)
    buffer_rows = experts * capacity
    target = jnp.arange(buffer_rows, dtype=jnp.int32)
    matches = (target[:, None, None] == slot_place[None, :, :]).astype(jnp.float32)
    select = jnp.sum(matches, axis=2)
    weighted = jnp.sum(matches * route_weights[None, :, :], axis=2)
    send_tokens = jnp.dot(
        select.astype(jnp.bfloat16), tokens, preferred_element_type=jnp.float32
    ).astype(jnp.bfloat16)
    send_grads = jnp.dot(
        weighted, out_grad.astype(jnp.float32), precision=lax.Precision.HIGHEST
    ).astype(jnp.bfloat16)
    recv_tokens, recv_grads = (
        lax.all_to_all(send_tokens, "expert", split_axis=0, concat_axis=0, tiled=True),
        lax.all_to_all(send_grads, "expert", split_axis=0, concat_axis=0, tiled=True),
    )
    buffer_shape = (sources, local_experts, capacity, width_dev)
    in_tokens = recv_tokens.reshape(buffer_shape)
    in_grads = recv_grads.reshape(buffer_shape)
    row_count = local_experts * sources * capacity
    gate_part = jnp.einsum(
        "sjcd,jdf->jscf", in_tokens, gate_weight, preferred_element_type=jnp.float32
    ).reshape(row_count, hidden_units)
    up_part = jnp.einsum(
        "sjcd,jdf->jscf", in_tokens, up_weight, preferred_element_type=jnp.float32
    ).reshape(row_count, hidden_units)
    back_part = jnp.einsum(
        "sjcd,jfd->jscf", in_grads, down_weight, preferred_element_type=jnp.float32
    ).reshape(row_count, hidden_units)
    gate_sum, up_sum, back_sum = (
        lax.psum_scatter(
            gate_part.astype(jnp.bfloat16), "dp", scatter_dimension=0, tiled=True
        ).astype(jnp.float32),
        lax.psum_scatter(
            up_part.astype(jnp.bfloat16), "dp", scatter_dimension=0, tiled=True
        ).astype(jnp.float32),
        lax.psum_scatter(
            back_part.astype(jnp.bfloat16), "dp", scatter_dimension=0, tiled=True
        ).astype(jnp.float32),
    )
    hidden, gate_delta, up_delta = swiglu_parts(gate_sum, up_sum, back_sum)
    hidden, gate_delta, up_delta = (
        lax.all_gather(hidden, "dp", axis=0, tiled=True),
        lax.all_gather(gate_delta, "dp", axis=0, tiled=True),
        lax.all_gather(up_delta, "dp", axis=0, tiled=True),
    )
    expert_shape = (local_experts, sources, capacity, hidden_units)
    hidden = hidden.reshape(expert_shape)
    gate_delta = gate_delta.reshape(expert_shape)
    up_delta = up_delta.reshape(expert_shape)
    expert_out = jnp.einsum(
        "jscf,jfd->sjcd", hidden, down_weight, preferred_element_type=jnp.float32
    ).astype(jnp.bfloat16)
    expert_back = (
        jnp.einsum("jscf,jdf->sjcd", gate_delta, gate_weight, preferred_element_type=jnp.float32)
        + jnp.einsum("jscf,jdf->sjcd", up_delta, up_weight, preferred_element_type=jnp.float32)
    ).astype(jnp.bfloat16)
    gate_grad = jnp.einsum(
        "sjcd,jscf->jdf", in_tokens, gate_delta, preferred_element_type=jnp.float32
    ).astype(jnp.bfloat16)
    up_grad = jnp.einsum(
        "sjcd,jscf->jdf", in_tokens, up_delta, preferred_element_type=jnp.float32
    ).astype(jnp.bfloat16)
    down_grad = jnp.einsum(
        "jscf,sjcd->jfd", hidden, in_grads, preferred_element_type=jnp.float32
    ).astype(jnp.bfloat16)
    out_back, grad_back = (
        lax.all_to_all(
            expert_out.reshape(buffer_rows, width_dev),
            "expert",
            split_axis=0,
            concat_axis=0,
            tiled=True,
        ),
        lax.all_to_all(
            expert_back.reshape(buffer_rows, width_dev),
            "expert",
            split_axis=0,
            concat_axis=0,
            tiled=True,
        ),
    )
    picked_out = jnp.take(out_back, slot_place, axis=0).astype(jnp.float32)
    layer_out = jnp.sum(picked_out * route_weights[:, :, None], axis=1).astype(jnp.bfloat16)
    picked_back = jnp.take(grad_back, slot_place, axis=0).astype(jnp.float32)
    grad_tokens = jnp.sum(picked_back, axis=1).astype(jnp.bfloat16)
    return (layer_out, grad_tokens, gate_grad, up_grad, down_grad)


def solution(mesh):
    in_specs = (
        P("expert", "dp"),
        P("expert", "dp"),
        P("expert", None),
        P("expert", None),
        P("expert", "dp", None),
        P("expert", "dp", None),
        P("expert", None, "dp"),
    )
    out_specs = (
        P("expert", "dp"),
        P("expert", "dp"),
        P("expert", "dp", None),
        P("expert", "dp", None),
        P("expert", None, "dp"),
    )
    return jax.shard_map(local, mesh=mesh, in_specs=in_specs, out_specs=out_specs, check_vma=False)
```

profile of v0, /device:TPU:0, one launch (start us, length us, event | category | flops | bytes accessed | tf_op | source)
XLA Modules:
  0.0 306.5 jit_solution(516927008975861477)
XLA Ops:
  13.4 5.3 %all-to-all-start.2 = ((bf16[8,96,1024]{2,1,0:T(8,128)(2,1)}), bf16[8,96,1024]{2,1,0:T(8,128)(2,1)S(1)}, u32[]{:S(2)}, u32[]{:S(2)}) async-start(bf16[8,96,1024]{2,1,0:T(8,128)(2,1)} %bitcast.12), calls=%async_computation.4 | async-start | bytes 3145728 | tf_op jit(solution)/shard_map/all_to_all | solution.py:45
  20.5 19.3 %all-to-all-done.2 = bf16[8,96,1024]{2,1,0:T(8,128)(2,1)S(1)} async-done(((bf16[8,96,1024]{2,1,0:T(8,128)(2,1)}), bf16[8,96,1024]{2,1,0:T(8,128)(2,1)S(1)}, u32[]{:S(2)}, u32[]{:S(2)}) %all-to-all-start.2) | async-done | bytes 1572896 | tf_op jit(solution)/shard_map/all_to_all | solution.py:45
  39.8 4.3 %all-to-all-start = ((bf16[8,96,1024]{2,1,0:T(8,128)(2,1)}), bf16[8,96,1024]{2,1,0:T(8,128)(2,1)}, u32[]{:S(2)}, u32[]{:S(2)}) async-start(bf16[8,96,1024]{2,1,0:T(8,128)(2,1)} %bitcast), calls=%async_computation | async-start | bytes 3145728 | tf_op jit(solution)/shard_map/all_to_all | solution.py:44
  45.0 8.9 %fusion.21 = bf16[8,8,12,768]{3,2,1,0:T(8,128)(2,1)S(1)} fusion(bf16[8,768,1024]{2,1,0:T(8,128)(2,1)} %param.15, bf16[8,8,12,1024]{3,0,2,1:T(8,128)(2,1)S(1)} %bitcast.75), kind=kOutput, calls=%fused_computation.26 | convolution fusion | flops 1208549376 | bytes 15335424 | tf_op jit(solution)/shard_map/sjcd,jfd->jscf/dot_general | solution.py:57
  55.1 10.0 %all-to-all-done = bf16[8,96,1024]{2,1,0:T(8,128)(2,1)} async-done(((bf16[8,96,1024]{2,1,0:T(8,128)(2,1)}), bf16[8,96,1024]{2,1,0:T(8,128)(2,1)}, u32[]{:S(2)}, u32[]{:S(2)}) %all-to-all-start) | async-done | bytes 1572896 | tf_op jit(solution)/shard_map/all_to_all | solution.py:44
  67.4 8.7 %fusion.31 = bf16[8,8,12,768]{3,2,1,0:T(8,128)(2,1)} fusion(bf16[8,1024,768]{2,1,0:T(8,128)(2,1)} %param.14, bf16[8,8,12,1024]{3,0,2,1:T(8,128)(2,1)S(1)} %bitcast.71), kind=kOutput, calls=%fused_computation.28 | convolution fusion | flops 1208549376 | bytes 15335424 | tf_op jit(solution)/shard_map/sjcd,jdf->jscf/dot_general | solution.py:54
  76.1 3.2 %convert_element_type.89 = bf16[768,768]{1,0:T(8,128)(2,1)} reshape(bf16[8,8,12,768]{3,2,1,0:T(8,128)(2,1)} %fusion.31) | data formatting | bytes 2359296 | tf_op jit(solution)/shard_map/convert_element_type | solution.py:65
  79.5 8.2 %fusion.26 = bf16[8,8,12,768]{3,2,1,0:T(8,128)(2,1)} fusion(bf16[8,1024,768]{2,1,0:T(8,128)(2,1)} %param.13, bf16[8,8,12,1024]{3,0,2,1:T(8,128)(2,1)S(1)} %bitcast.72), kind=kOutput, calls=%fused_computation.27 | convolution fusion | flops 1208549376 | bytes 15335424 | tf_op jit(solution)/shard_map/sjcd,jdf->jscf/dot_general | solution.py:51
  87.7 3.1 %convert_element_type.86 = bf16[768,768]{1,0:T(8,128)(2,1)} reshape(bf16[8,8,12,768]{3,2,1,0:T(8,128)(2,1)} %fusion.26) | data formatting | bytes 2359296 | tf_op jit(solution)/shard_map/convert_element_type | solution.py:62
  90.9 25.8 %reduce-scatter.6.cloned.1.call-done = bf16[192,768]{1,0:T(8,128)(2,1)} async-done(((bf16[768,768]{1,0:T(8,128)(2,1)}), bf16[192,768]{1,0:T(8,128)(2,1)}) %reduce-scatter.6.cloned.1.call-update) | async-done | bytes 294928 | tf_op jit(solution)/shard_map/reduce_scatter | solution.py:64
  116.8 30.2 %reduce-scatter.4.cloned.1.call-done = bf16[192,768]{1,0:T(8,128)(2,1)} async-done(((bf16[768,768]{1,0:T(8,128)(2,1)}), bf16[192,768]{1,0:T(8,128)(2,1)}) %reduce-scatter.4.cloned.1.call-update) | async-done | bytes 294928 | tf_op jit(solution)/shard_map/reduce_scatter | solution.py:61
  151.5 27.2 %all-gather.4.cloned.1.call-done = bf16[768,768]{1,0:T(8,128)(2,1)} async-done(((bf16[192,768]{1,0:T(8,128)(2,1)}), bf16[768,768]{1,0:T(8,128)(2,1)}) %all-gather.4.cloned.1.call-update) | async-done | bytes 1179664 | tf_op jit(solution)/shard_map/all_gather | solution.py:73
  180.9 6.8 %bitcast_convert_fusion = bf16[8,768,1024]{2,1,0:T(8,128)(2,1)} fusion(bf16[8,8,12,768]{3,2,1,0:T(8,128)(2,1)S(1)} %reshape.64, bf16[8,8,12,1024]{3,0,2,1:T(8,128)(2,1)S(1)} %bitcast.76), kind=kOutput, calls=%fused_computation.2 | convolution fusion | flops 1214251008 | bytes 15335424 | tf_op jit(solution)/shard_map/jscf,sjcd->jfd/dot_general | solution.py:94
  187.7 6.4 %convert_bitcast_fusion = bf16[8,8,12,1024]{3,2,0,1:T(8,128)(2,1)S(1)} fusion(bf16[8,8,12,768]{3,2,1,0:T(8,128)(2,1)S(1)} %reshape.64, bf16[8,768,1024]{2,1,0:T(8,128)(2,1)} %param.15), kind=kOutput, calls=%fused_computation.23 | convolution fusion | flops 1208745984 | bytes 15335424 | tf_op jit(solution)/shard_map/jscf,jfd->sjcd/dot_general | solution.py:81
  197.0 4.5 %all-to-all-start.1 = ((bf16[8,96,1024]{2,1,0:T(8,128)(2,1)}), bf16[8,96,1024]{2,1,0:T(8,128)(2,1)}, u32[]{:S(2)}, u32[]{:S(2)}) async-start(bf16[8,96,1024]{2,1,0:T(8,128)(2,1)} %copy.76), calls=%async_computation.3 | async-start | bytes 3145728 | tf_op jit(solution)/shard_map/all_to_all | solution.py:98
  201.5 8.8 %all-gather.8.cloned.1.call-done = bf16[768,768]{1,0:T(8,128)(2,1)} async-done(((bf16[192,768]{1,0:T(8,128)(2,1)}), bf16[768,768]{1,0:T(8,128)(2,1)}) %all-gather.8.cloned.1.call-update) | async-done | bytes 1179664 | tf_op jit(solution)/shard_map/all_gather | solution.py:75
  212.5 11.2 %fusion = f32[8,8,12,1024]{3,2,1,0:T(8,128)} fusion(bf16[8,8,12,768]{3,2,1,0:T(8,128)(2,1)S(1)} %reshape.67, bf16[8,1024,768]{2,1,0:T(8,128)(2,1)} %param.14), kind=kOutput, calls=%fused_computation.5 | convolution fusion | flops 1207959552 | bytes 16908288 | tf_op jit(solution)/shard_map/jscf,jdf->sjcd/dot_general | solution.py:86
  223.7 18.2 %all-gather.6.cloned.1.call-done = bf16[768,768]{1,0:T(8,128)(2,1)} async-done(((bf16[192,768]{1,0:T(8,128)(2,1)}), bf16[768,768]{1,0:T(8,128)(2,1)}) %all-gather.6.cloned.1.call-update) | async-done | bytes 1179664 | tf_op jit(solution)/shard_map/all_gather | solution.py:74
  245.0 10.3 %bitcast_convert_fusion.2 = bf16[8,1024,768]{2,1,0:T(8,128)(2,1)} fusion(bf16[8,8,12,1024]{3,0,2,1:T(8,128)(2,1)} %bitcast.73, bf16[8,8,12,768]{3,2,1,0:T(8,128)(2,1)} %reshape.66), kind=kOutput, calls=%fused_computation.4 | convolution fusion | flops 1214251008 | bytes 15335424 | tf_op jit(solution)/shard_map/sjcd,jscf->jdf/dot_general | solution.py:88
  255.3 10.6 %fusion.16 = bf16[8,8,12,1024]{3,2,0,1:T(8,128)(2,1)} fusion(f32[8,8,12,1024]{3,2,1,0:T(8,128)S(1)} %copy-done.2, bf16[8,8,12,768]{3,2,1,0:T(8,128)(2,1)} %reshape.66, bf16[8,1024,768]{2,1,0:T(8,128)(2,1)} %param.13), kind=kOutput, calls=%fused_computation.22 | convolution fusion | flops 1209532416 | bytes 18481152 | tf_op jit(solution)/shard_map/jscf,jdf->sjcd/dot_general | solution.py:85
  270.4 4.0 %all-to-all-start.3 = ((bf16[8,96,1024]{2,1,0:T(8,128)(2,1)}), bf16[8,96,1024]{2,1,0:T(8,128)(2,1)S(1)}, u32[]{:S(2)}, u32[]{:S(2)}) async-start(bf16[8,96,1024]{2,1,0:T(8,128)(2,1)} %copy.84), calls=%async_computation.6 | async-start | bytes 3145728 | tf_op jit(solution)/shard_map/all_to_all | solution.py:105
  274.4 8.0 %bitcast_convert_fusion.1 = bf16[8,1024,768]{2,1,0:T(8,128)(2,1)} fusion(bf16[8,8,12,1024]{3,0,2,1:T(8,128)(2,1)S(1)} %bitcast.74, bf16[8,8,12,768]{3,2,1,0:T(8,128)(2,1)} %copy-done.5), kind=kOutput, calls=%fused_computation.3 | convolution fusion | flops 1214251008 | bytes 15335424 | tf_op jit(solution)/shard_map/sjcd,jscf->jdf/dot_general | solution.py:91
  282.4 4.4 %gather_fusion = bf16[384,1024]{1,0:T(8,128)(2,1)S(1)} fusion(bf16[768,1024]{1,0:T(8,128)(2,1)} %bitcast.10, s32[1024]{0:T(1024)S(1)} %copy-done.6), kind=kCustom, calls=%fused_computation.clone | custom fusion | bytes 1574400 | tf_op jit(solution)/shard_map/jit(_take)/gather | solution.py:113
  286.8 8.4 %all-to-all-done.3 = bf16[8,96,1024]{2,1,0:T(8,128)(2,1)S(1)} async-done(((bf16[8,96,1024]{2,1,0:T(8,128)(2,1)}), bf16[8,96,1024]{2,1,0:T(8,128)(2,1)S(1)}, u32[]{:S(2)}, u32[]{:S(2)}) %all-to-all-start.3) | async-done | bytes 1572896 | tf_op jit(solution)/shard_map/all_to_all | solution.py:105
  (66 shorter events, 36.5 us)
Async XLA Ops:
  7.2 3.7 %copy-start = (bf16[48,1024]{1,0:T(8,128)(2,1)S(1)}, bf16[48,1024]{1,0:T(8,128)(2,1)}, u32[]{:S(2)}) copy-start(bf16[48,1024]{1,0:T(8,128)(2,1)} %param.10) | copy-start | bytes 294916
  8.0 5.4 %copy-start.7 = (f32[48,8]{1,0:T(8,128)}, f32[48,8]{1,0:T(8,128)S(1)}, u32[]{:S(2)}) copy-start(f32[48,8]{1,0:T(8,128)S(1)} %copy.78) | copy-start | bytes 4612
  13.4 5.3 %copy-start.9 = (bf16[48,1024]{1,0:T(8,128)(2,1)S(1)}, bf16[48,1024]{1,0:T(8,128)(2,1)}, u32[]{:S(2)}) copy-start(bf16[48,1024]{1,0:T(8,128)(2,1)} %param.9) | copy-start | bytes 294916
  13.4 26.3 %all-to-all-start.2 = ((bf16[8,96,1024]{2,1,0:T(8,128)(2,1)}), bf16[8,96,1024]{2,1,0:T(8,128)(2,1)S(1)}, u32[]{:S(2)}, u32[]{:S(2)}) async-start(bf16[8,96,1024]{2,1,0:T(8,128)(2,1)} %bitcast.12), calls=%async_computation.4 | async-start | bytes 3145728 | tf_op jit(solution)/shard_map/all_to_all | solution.py:45
  39.8 25.3 %all-to-all-start = ((bf16[8,96,1024]{2,1,0:T(8,128)(2,1)}), bf16[8,96,1024]{2,1,0:T(8,128)(2,1)}, u32[]{:S(2)}, u32[]{:S(2)}) async-start(bf16[8,96,1024]{2,1,0:T(8,128)(2,1)} %bitcast), calls=%async_computation | async-start | bytes 3145728 | tf_op jit(solution)/shard_map/all_to_all | solution.py:44
  44.1 46.9 %reduce-scatter.8.cloned.1.call-start = ((), (), s32[]{:S(2)}) async-start(), calls=%async_computation.10 | async-start | bytes 1474560 | tf_op jit(solution)/shard_map/reduce_scatter | solution.py:67
  55.1 61.7 %reduce-scatter.6.cloned.1.call-start = ((), (), s32[]{:S(2)}) async-start(), calls=%async_computation.8 | async-start | bytes 1474560 | tf_op jit(solution)/shard_map/reduce_scatter | solution.py:64
  67.4 12.1 %copy-start.3 = (bf16[8,96,1024]{2,0,1:T(8,128)(2,1)}, bf16[8,96,1024]{2,0,1:T(8,128)(2,1)S(1)}, u32[]{:S(2)}) copy-start(bf16[8,96,1024]{2,0,1:T(8,128)(2,1)S(1)} %copy.72) | copy-start | bytes 4718596
  79.3 67.7 %reduce-scatter.4.cloned.1.call-start = ((), (), s32[]{:S(2)}) async-start(), calls=%async_computation.7 | async-start | bytes 1474560 | tf_op jit(solution)/shard_map/reduce_scatter | solution.py:61
  90.9 87.9 %all-gather.4.cloned.1.call-start = ((), (), s32[]{:S(2)}) async-start(), calls=%async_computation.9 | async-start | bytes 1474560 | tf_op jit(solution)/shard_map/all_gather | solution.py:73
  149.4 60.9 %all-gather.8.cloned.1.call-start = ((), (), s32[]{:S(2)}) async-start(), calls=%async_computation.12 | async-start | bytes 1474560 | tf_op jit(solution)/shard_map/all_gather | solution.py:75
  150.0 91.9 %all-gather.6.cloned.1.call-start = ((), (), s32[]{:S(2)}) async-start(), calls=%async_computation.11 | async-start | bytes 1474560 | tf_op jit(solution)/shard_map/all_gather | solution.py:74
  197.0 73.4 %all-to-all-start.1 = ((bf16[8,96,1024]{2,1,0:T(8,128)(2,1)}), bf16[8,96,1024]{2,1,0:T(8,128)(2,1)}, u32[]{:S(2)}, u32[]{:S(2)}) async-start(bf16[8,96,1024]{2,1,0:T(8,128)(2,1)} %copy.76), calls=%async_computation.3 | async-start | bytes 3145728 | tf_op jit(solution)/shard_map/all_to_all | solution.py:98
  212.5 11.2 %copy-start.5 = (bf16[8,8,12,768]{3,2,1,0:T(8,128)(2,1)}, bf16[8,8,12,768]{3,2,1,0:T(8,128)(2,1)S(1)}, u32[]{:S(2)}) copy-start(bf16[8,8,12,768]{3,2,1,0:T(8,128)(2,1)S(1)} %reshape.67) | copy-start | bytes 3538948
  245.0 10.3 %copy-start.2 = (f32[8,8,12,1024]{3,2,1,0:T(8,128)S(1)}, f32[8,8,12,1024]{3,2,1,0:T(8,128)}, u32[]{:S(2)}) copy-start(f32[8,8,12,1024]{3,2,1,0:T(8,128)} %fusion) | copy-start | bytes 9437188
  270.4 4.0 %copy-start.4 = (bf16[8,96,1024]{2,0,1:T(8,128)(2,1)S(1)}, bf16[8,96,1024]{2,0,1:T(8,128)(2,1)}, u32[]{:S(2)}) copy-start(bf16[8,96,1024]{2,0,1:T(8,128)(2,1)} %copy-done.3) | copy-start | bytes 4718596
  270.4 24.8 %all-to-all-start.3 = ((bf16[8,96,1024]{2,1,0:T(8,128)(2,1)}), bf16[8,96,1024]{2,1,0:T(8,128)(2,1)S(1)}, u32[]{:S(2)}, u32[]{:S(2)}) async-start(bf16[8,96,1024]{2,1,0:T(8,128)(2,1)} %copy.84), calls=%async_computation.6 | async-start | bytes 3145728 | tf_op jit(solution)/shard_map/all_to_all | solution.py:105
  274.4 8.1 %copy-start.6 = (s32[1024]{0:T(1024)S(1)}, s32[1024]{0:T(1024)}, u32[]{:S(2)}) copy-start(s32[1024]{0:T(1024)} %pad_clamp_fusion) | copy-start | bytes 12292
  295.2 2.1 copy-start.8
  295.2 2.1 copy-start.10
  295.2 4.4 %copy-start.1 = (bf16[48,1024]{1,0:T(8,128)(2,1)S(1)}, bf16[48,1024]{1,0:T(8,128)(2,1)}, u32[]{:S(2)}) copy-start(bf16[48,1024]{1,0:T(8,128)(2,1)} %param.10) | copy-start | bytes 294916
Sparse Core Ops, SparseCore 0:
  55.2 30.7 reduce-scatter.7
  88.8 27.8 reduce-scatter.5
  119.1 27.8 reduce-scatter.3
  149.5 29.1 all-gather.3
  180.7 29.5 all-gather.7
  212.3 29.5 all-gather.5
where the time goes:
time: 308 us; the launch traced here: 306 us
  waiting for transfers between devices  149 us (48%)
  matrix products  83.4 us (27%)
  local copies, waits for them, and re-layouts  34.7 us (11%)
  starting transfers between devices  18.5 us (6%)
  between operations  14.3 us (5%)
  other arithmetic  7.03 us (2%)
    reduce_scatter x1, waiting for transfers between devices, local(): lax.psum_scatter(gate_part.astype(jnp.bfloat16), 'dp', scatter_dimension=...  30.2 us
    all_gather x1, waiting for transfers between devices, local(): lax.all_gather(hidden, 'dp', axis=0, tiled=True)  27.2 us
    reduce_scatter x1, waiting for transfers between devices, local(): lax.psum_scatter(up_part.astype(jnp.bfloat16), 'dp', scatter_dimension=0,...  25.8 us
    all_to_all x1, waiting for transfers between devices, local(): lax.all_to_all(send_grads, 'expert', split_axis=0, concat_axis=0, tiled=T...  19.3 us
    all_gather x1, waiting for transfers between devices, local(): lax.all_gather(gate_delta, 'dp', axis=0, tiled=True)  18.2 us
    dot_general x1, matrix products, local(): jnp.einsum('jscf,jdf->sjcd', up_delta, up_weight, preferred_element_type=...  11.2 us
    dot_general x1, matrix products, local(): jnp.einsum('jscf,jdf->sjcd', gate_delta, gate_weight, preferred_element_t...  10.6 us
    dot_general x1, matrix products, local(): jnp.einsum('sjcd,jscf->jdf', in_tokens, gate_delta, preferred_element_typ...  10.3 us
  transfers between devices with their start and end apart: 10, of which 8 were waited for; matrix products, arithmetic and copies ran while one was open for 37% of the time, Pallas kernels for 0%

commit v1 on v0

--- a/solution.py
+++ b/solution.py
@@ -2,6 +2,23 @@
 import jax.numpy as jnp
 from jax import lax
 from jax.sharding import PartitionSpec as P
+
+
+def laid_out(blocks, dim):
+    blocks = jnp.moveaxis(blocks, 0, dim)
+    lengths = blocks.shape
+    return blocks.reshape(*lengths[:dim], lengths[dim] * lengths[dim + 1], *lengths[dim + 2 :])
+
+
+def gather_around(x, axis, dim):
+    peers = lax.axis_size(axis)
+    right = [(i, (i + 1) % peers) for i in range(peers)]
+    pieces = [x]
+    while len(pieces) < peers:
+        pieces.append(lax.ppermute(pieces[-1], axis, right))
+    here = lax.axis_index(axis)
+    pieces = jnp.stack(pieces)[(here - jnp.arange(peers)) % peers]
+    return laid_out(pieces, dim)
 
 
 def swiglu_parts(gate_sum, up_sum, back_sum):
@@ -71,7 +88,7 @@
     hidden, gate_delta, up_delta = swiglu_parts(gate_sum, up_sum, back_sum)
     hidden, gate_delta, up_delta = (
         lax.all_gather(hidden, "dp", axis=0, tiled=True),
-        lax.all_gather(gate_delta, "dp", axis=0, tiled=True),
+        gather_around(gate_delta, "dp", 0),
         lax.all_gather(up_delta, "dp", axis=0, tiled=True),
     )
     expert_shape = (local_experts, sources, capacity, hidden_units)

time: 308 us -> 296 us (0.961)
  waiting for transfers between devices: 149 us -> 134 us
  matrix products: 83.4 us -> 79 us
  local copies, waits for them, and re-layouts: 34.7 us -> 38.6 us
    ppermute x0 -> x3, waiting for transfers between devices: none -> 40 us  [gather_around(): pieces.append(lax.ppermute(pieces[-1], axis, right))]
    all_gather x1, waiting for transfers between devices: 27.2 us -> 0.01 us  [local(): lax.all_gather(hidden, 'dp', axis=0, tiled=True)]
    all_gather x1 -> x0, waiting for transfers between devices: 18.2 us -> none  [local(): lax.all_gather(gate_delta, 'dp', axis=0, tiled=True)]
    all_gather x1, waiting for transfers between devices: 8.77 us -> 0.02 us  [local(): lax.all_gather(up_delta, 'dp', axis=0, tiled=True)]
    another operation x0 -> x1, local copies, waits for them, and re-layouts: none -> 3.15 us  [local(): gate_delta = gate_delta.reshape(expert_shape)]
    reshape x1 -> x0, local copies, waits for them, and re-layouts: 3.12 us -> none  [local(): gate_delta = gate_delta.reshape(expert_shape)]
  transfers between devices with their start and end apart: 10 -> 12, of which waited for: 8 -> 8; matrix products, arithmetic and copies ran while one was open for 37% -> 39% of each run, Pallas kernels for 0% -> 0%
where the time goes in v1:
time: 296 us; the launch traced here: 295 us
  waiting for transfers between devices  134 us (45%)
  matrix products  79 us (27%)
  local copies, waits for them, and re-layouts  38.6 us (13%)
  starting transfers between devices  19.6 us (7%)
  between operations  14 us (5%)
  other arithmetic  9.31 us (3%)
    ppermute x3, waiting for transfers between devices, gather_around(): pieces.append(lax.ppermute(pieces[-1], axis, right))  40 us
    reduce_scatter x1, waiting for transfers between devices, local(): lax.psum_scatter(gate_part.astype(jnp.bfloat16), 'dp', scatter_dimension=...  30.2 us
    reduce_scatter x1, waiting for transfers between devices, local(): lax.psum_scatter(up_part.astype(jnp.bfloat16), 'dp', scatter_dimension=0,...  25.9 us
    all_to_all x1, waiting for transfers between devices, local(): lax.all_to_all(send_grads, 'expert', split_axis=0, concat_axis=0, tiled=T...  19.3 us
    dot_general x1, matrix products, local(): jnp.einsum('jscf,jdf->sjcd', gate_delta, gate_weight, preferred_element_t...  10.6 us
    all_to_all x1, waiting for transfers between devices, local(): lax.all_to_all(send_tokens, 'expert', split_axis=0, concat_axis=0, tiled=...  9.99 us
    dot_general x1, matrix products, local(): jnp.einsum('jscf,jdf->sjcd', up_delta, up_weight, preferred_element_type=...  9.12 us
    dot_general x1, matrix products, local(): jnp.einsum('sjcd,jfd->jscf', in_grads, down_weight, preferred_element_typ...  8.88 us
  transfers between devices with their start and end apart: 12, of which 8 were waited for; matrix products, arithmetic and copies ran while one was open for 39% of the time, Pallas kernels for 0%

profile of v1, /device:TPU:0, one launch (start us, length us, event | category | flops | bytes accessed | tf_op | source)
XLA Modules:
  0.0 294.6 jit_solution(16048921670996724207)
XLA Ops:
  13.4 5.3 %all-to-all-start.2 = ((bf16[8,96,1024]{2,1,0:T(8,128)(2,1)}), bf16[8,96,1024]{2,1,0:T(8,128)(2,1)S(1)}, u32[]{:S(2)}, u32[]{:S(2)}) async-start(bf16[8,96,1024]{2,1,0:T(8,128)(2,1)} %bitcast.12), calls=%async_computation.4 | async-start | bytes 3145728 | tf_op jit(solution)/shard_map/all_to_all | solution.py:62
  20.5 19.3 %all-to-all-done.2 = bf16[8,96,1024]{2,1,0:T(8,128)(2,1)S(1)} async-done(((bf16[8,96,1024]{2,1,0:T(8,128)(2,1)}), bf16[8,96,1024]{2,1,0:T(8,128)(2,1)S(1)}, u32[]{:S(2)}, u32[]{:S(2)}) %all-to-all-start.2) | async-done | bytes 1572896 | tf_op jit(solution)/shard_map/all_to_all | solution.py:62
  39.8 4.3 %all-to-all-start = ((bf16[8,96,1024]{2,1,0:T(8,128)(2,1)}), bf16[8,96,1024]{2,1,0:T(8,128)(2,1)}, u32[]{:S(2)}, u32[]{:S(2)}) async-start(bf16[8,96,1024]{2,1,0:T(8,128)(2,1)} %bitcast), calls=%async_computation | async-start | bytes 3145728 | tf_op jit(solution)/shard_map/all_to_all | solution.py:61
  45.0 8.9 %fusion.21 = bf16[8,8,12,768]{3,2,1,0:T(8,128)(2,1)S(1)} fusion(bf16[8,768,1024]{2,1,0:T(8,128)(2,1)} %param.15, bf16[8,8,12,1024]{3,0,2,1:T(8,128)(2,1)S(1)} %bitcast.81), kind=kOutput, calls=%fused_computation.27 | convolution fusion | flops 1208549376 | bytes 15335424 | tf_op jit(solution)/shard_map/sjcd,jfd->jscf/dot_general | solution.py:74
  55.1 10.0 %all-to-all-done = bf16[8,96,1024]{2,1,0:T(8,128)(2,1)} async-done(((bf16[8,96,1024]{2,1,0:T(8,128)(2,1)}), bf16[8,96,1024]{2,1,0:T(8,128)(2,1)}, u32[]{:S(2)}, u32[]{:S(2)}) %all-to-all-start) | async-done | bytes 1572896 | tf_op jit(solution)/shard_map/all_to_all | solution.py:61
  67.4 8.7 %fusion.31 = bf16[8,8,12,768]{3,2,1,0:T(8,128)(2,1)} fusion(bf16[8,1024,768]{2,1,0:T(8,128)(2,1)} %param.14, bf16[8,8,12,1024]{3,0,2,1:T(8,128)(2,1)S(1)} %bitcast.77), kind=kOutput, calls=%fused_computation.29 | convolution fusion | flops 1208549376 | bytes 15335424 | tf_op jit(solution)/shard_map/sjcd,jdf->jscf/dot_general | solution.py:71
  76.1 3.2 %convert_element_type.89 = bf16[768,768]{1,0:T(8,128)(2,1)} reshape(bf16[8,8,12,768]{3,2,1,0:T(8,128)(2,1)} %fusion.31) | data formatting | bytes 2359296 | tf_op jit(solution)/shard_map/convert_element_type | solution.py:82
  79.5 8.2 %fusion.26 = bf16[8,8,12,768]{3,2,1,0:T(8,128)(2,1)} fusion(bf16[8,1024,768]{2,1,0:T(8,128)(2,1)} %param.13, bf16[8,8,12,1024]{3,0,2,1:T(8,128)(2,1)S(1)} %bitcast.78), kind=kOutput, calls=%fused_computation.28 | convolution fusion | flops 1208549376 | bytes 15335424 | tf_op jit(solution)/shard_map/sjcd,jdf->jscf/dot_general | solution.py:68
  90.9 25.9 %reduce-scatter.6.cloned.1.call-done = bf16[192,768]{1,0:T(8,128)(2,1)} async-done(((bf16[768,768]{1,0:T(8,128)(2,1)}), bf16[192,768]{1,0:T(8,128)(2,1)}) %reduce-scatter.6.cloned.1.call-update) | async-done | bytes 294928 | tf_op jit(solution)/shard_map/reduce_scatter | solution.py:81
  116.8 30.2 %reduce-scatter.4.cloned.1.call-done = bf16[192,768]{1,0:T(8,128)(2,1)} async-done(((bf16[768,768]{1,0:T(8,128)(2,1)}), bf16[192,768]{1,0:T(8,128)(2,1)}) %reduce-scatter.4.cloned.1.call-update) | async-done | bytes 294928 | tf_op jit(solution)/shard_map/reduce_scatter | solution.py:78
  149.5 10.6 %collective-permute-done = bf16[192,768]{1,0:T(8,128)(2,1)} collective-permute-done((bf16[192,768]{1,0:T(8,128)(2,1)S(1)}, bf16[192,768]{1,0:T(8,128)(2,1)}, u32[]{:S(2)}, u32[]{:S(2)}) %collective-permute-start) | collective-permute-done | bytes 294944 | tf_op jit(solution)/shard_map/ppermute | solution.py:18
  161.0 16.7 %collective-permute-done.1 = bf16[192,768]{1,0:T(8,128)(2,1)} collective-permute-done((bf16[192,768]{1,0:T(8,128)(2,1)}, bf16[192,768]{1,0:T(8,128)(2,1)}, u32[]{:S(2)}, u32[]{:S(2)}) %collective-permute-start.1) | collective-permute-done | bytes 294944 | tf_op jit(solution)/shard_map/ppermute | solution.py:18
  179.3 12.7 %collective-permute-done.2 = bf16[192,768]{1,0:T(8,128)(2,1)} collective-permute-done((bf16[192,768]{1,0:T(8,128)(2,1)}, bf16[192,768]{1,0:T(8,128)(2,1)}, u32[]{:S(2)}, u32[]{:S(2)}) %collective-permute-start.2) | collective-permute-done | bytes 294944 | tf_op jit(solution)/shard_map/ppermute | solution.py:18
  197.2 3.1 %reshape_reshape.3 = bf16[8,8,12,768]{3,2,1,0:T(8,128)(2,1)} reshape(bf16[4,192,768]{2,1,0:T(8,128)(2,1)} %gather_fusion) | data formatting | bytes 2359296 | tf_op jit(solution)/shard_map/reshape;reshape | solution.py:96
  200.4 8.0 %bitcast_convert_fusion.2 = bf16[8,1024,768]{2,1,0:T(8,128)(2,1)} fusion(bf16[8,8,12,1024]{3,0,2,1:T(8,128)(2,1)S(1)} %bitcast.79, bf16[8,8,12,768]{3,2,1,0:T(8,128)(2,1)} %reshape_reshape.3), kind=kOutput, calls=%fused_computation.5 | convolution fusion | flops 1214251008 | bytes 15335424 | tf_op jit(solution)/shard_map/sjcd,jscf->jdf/dot_general | solution.py:105
  210.6 6.8 %bitcast_convert_fusion = bf16[8,768,1024]{2,1,0:T(8,128)(2,1)} fusion(bf16[8,8,12,768]{3,2,1,0:T(8,128)(2,1)S(1)} %reshape.110, bf16[8,8,12,1024]{3,0,2,1:T(8,128)(2,1)S(1)} %bitcast.82), kind=kOutput, calls=%fused_computation.3 | convolution fusion | flops 1214251008 | bytes 15335424 | tf_op jit(solution)/shard_map/jscf,sjcd->jfd/dot_general | solution.py:111
  217.3 6.4 %convert_bitcast_fusion = bf16[8,8,12,1024]{3,2,0,1:T(8,128)(2,1)S(1)} fusion(bf16[8,8,12,768]{3,2,1,0:T(8,128)(2,1)S(1)} %reshape.110, bf16[8,768,1024]{2,1,0:T(8,128)(2,1)} %param.15), kind=kOutput, calls=%fused_computation.24 | convolution fusion | flops 1208745984 | bytes 15335424 | tf_op jit(solution)/shard_map/jscf,jfd->sjcd/dot_general | solution.py:98
  226.7 4.5 %all-to-all-start.1 = ((bf16[8,96,1024]{2,1,0:T(8,128)(2,1)}), bf16[8,96,1024]{2,1,0:T(8,128)(2,1)}, u32[]{:S(2)}, u32[]{:S(2)}) async-start(bf16[8,96,1024]{2,1,0:T(8,128)(2,1)} %copy.76), calls=%async_computation.3 | async-start | bytes 3145728 | tf_op jit(solution)/shard_map/all_to_all | solution.py:115
  234.4 9.1 %fusion = f32[8,8,12,1024]{3,2,1,0:T(8,128)S(1)} fusion(bf16[8,8,12,768]{3,2,1,0:T(8,128)(2,1)} %reshape.112, bf16[8,1024,768]{2,1,0:T(8,128)(2,1)} %param.14), kind=kOutput, calls=%fused_computation.6 | convolution fusion | flops 1207959552 | bytes 16908288 | tf_op jit(solution)/shard_map/jscf,jdf->sjcd/dot_general | solution.py:103
  243.5 10.6 %fusion.16 = bf16[8,8,12,1024]{3,2,0,1:T(8,128)(2,1)} fusion(f32[8,8,12,1024]{3,2,1,0:T(8,128)S(1)} %fusion, bf16[8,8,12,768]{3,2,1,0:T(8,128)(2,1)} %reshape_reshape.3, bf16[8,1024,768]{2,1,0:T(8,128)(2,1)} %param.13), kind=kOutput, calls=%fused_computation.23 | convolution fusion | flops 1209532416 | bytes 18481152 | tf_op jit(solution)/shard_map/jscf,jdf->sjcd/dot_general | solution.py:102
  258.6 4.0 %all-to-all-start.3 = ((bf16[8,96,1024]{2,1,0:T(8,128)(2,1)}), bf16[8,96,1024]{2,1,0:T(8,128)(2,1)S(1)}, u32[]{:S(2)}, u32[]{:S(2)}) async-start(bf16[8,96,1024]{2,1,0:T(8,128)(2,1)} %copy.84), calls=%async_computation.6 | async-start | bytes 3145728 | tf_op jit(solution)/shard_map/all_to_all | solution.py:122
  262.6 8.0 %bitcast_convert_fusion.1 = bf16[8,1024,768]{2,1,0:T(8,128)(2,1)} fusion(bf16[8,8,12,1024]{3,0,2,1:T(8,128)(2,1)S(1)} %bitcast.80, bf16[8,8,12,768]{3,2,1,0:T(8,128)(2,1)} %reshape.112), kind=kOutput, calls=%fused_computation.4 | convolution fusion | flops 1214251008 | bytes 15335424 | tf_op jit(solution)/shard_map/sjcd,jscf->jdf/dot_general | solution.py:108
  270.6 4.4 %gather_fusion.1 = bf16[384,1024]{1,0:T(8,128)(2,1)S(1)} fusion(bf16[768,1024]{1,0:T(8,128)(2,1)} %bitcast.10, s32[1024]{0:T(1024)S(1)} %copy-done.4), kind=kCustom, calls=%fused_computation.clone | custom fusion | bytes 1574400 | tf_op jit(solution)/shard_map/jit(_take)/gather | solution.py:130
  275.0 8.6 %all-to-all-done.3 = bf16[8,96,1024]{2,1,0:T(8,128)(2,1)S(1)} async-done(((bf16[8,96,1024]{2,1,0:T(8,128)(2,1)}), bf16[8,96,1024]{2,1,0:T(8,128)(2,1)S(1)}, u32[]{:S(2)}, u32[]{:S(2)}) %all-to-all-start.3) | async-done | bytes 1572896 | tf_op jit(solution)/shard_map/all_to_all | solution.py:122
  (69 shorter events, 43.2 us)
Async XLA Ops:
  7.2 3.7 %copy-start = (bf16[48,1024]{1,0:T(8,128)(2,1)S(1)}, bf16[48,1024]{1,0:T(8,128)(2,1)}, u32[]{:S(2)}) copy-start(bf16[48,1024]{1,0:T(8,128)(2,1)} %param.10) | copy-start | bytes 294916
  8.0 5.4 %copy-start.5 = (f32[48,8]{1,0:T(8,128)}, f32[48,8]{1,0:T(8,128)S(1)}, u32[]{:S(2)}) copy-start(f32[48,8]{1,0:T(8,128)S(1)} %copy.78) | copy-start | bytes 4612
  13.4 5.3 %copy-start.7 = (bf16[48,1024]{1,0:T(8,128)(2,1)S(1)}, bf16[48,1024]{1,0:T(8,128)(2,1)}, u32[]{:S(2)}) copy-start(bf16[48,1024]{1,0:T(8,128)(2,1)} %param.9) | copy-start | bytes 294916
  13.4 26.3 %all-to-all-start.2 = ((bf16[8,96,1024]{2,1,0:T(8,128)(2,1)}), bf16[8,96,1024]{2,1,0:T(8,128)(2,1)S(1)}, u32[]{:S(2)}, u32[]{:S(2)}) async-start(bf16[8,96,1024]{2,1,0:T(8,128)(2,1)} %bitcast.12), calls=%async_computation.4 | async-start | bytes 3145728 | tf_op jit(solution)/shard_map/all_to_all | solution.py:62
  39.8 25.4 %all-to-all-start = ((bf16[8,96,1024]{2,1,0:T(8,128)(2,1)}), bf16[8,96,1024]{2,1,0:T(8,128)(2,1)}, u32[]{:S(2)}, u32[]{:S(2)}) async-start(bf16[8,96,1024]{2,1,0:T(8,128)(2,1)} %bitcast), calls=%async_computation | async-start | bytes 3145728 | tf_op jit(solution)/shard_map/all_to_all | solution.py:61
  44.1 46.8 %reduce-scatter.8.cloned.1.call-start = ((), (), s32[]{:S(2)}) async-start(), calls=%async_computation.10 | async-start | bytes 1474560 | tf_op jit(solution)/shard_map/reduce_scatter | solution.py:84
  55.1 61.7 %reduce-scatter.6.cloned.1.call-start = ((), (), s32[]{:S(2)}) async-start(), calls=%async_computation.8 | async-start | bytes 1474560 | tf_op jit(solution)/shard_map/reduce_scatter | solution.py:81
  67.4 133.0 %copy-start.2 = (bf16[8,96,1024]{2,0,1:T(8,128)(2,1)}, bf16[8,96,1024]{2,0,1:T(8,128)(2,1)S(1)}, u32[]{:S(2)}) copy-start(bf16[8,96,1024]{2,0,1:T(8,128)(2,1)S(1)} %copy.72) | copy-start | bytes 4718596
  79.3 67.7 %reduce-scatter.4.cloned.1.call-start = ((), (), s32[]{:S(2)}) async-start(), calls=%async_computation.7 | async-start | bytes 1474560 | tf_op jit(solution)/shard_map/reduce_scatter | solution.py:78
  90.8 117.6 %all-gather.3.cloned.1.call-start = ((), (), s32[]{:S(2)}) async-start(), calls=%async_computation.9 | async-start | bytes 1474560 | tf_op jit(solution)/shard_map/all_gather | solution.py:90
  149.4 81.8 %all-gather.5.cloned.1.call-start = ((), (), s32[]{:S(2)}) async-start(), calls=%async_computation.11 | async-start | bytes 1474560 | tf_op jit(solution)/shard_map/all_gather | solution.py:92
  149.4 10.7 %collective-permute-start = (bf16[192,768]{1,0:T(8,128)(2,1)S(1)}, bf16[192,768]{1,0:T(8,128)(2,1)}, u32[]{:S(2)}, u32[]{:S(2)}) collective-permute-start(bf16[192,768]{1,0:T(8,128)(2,1)S(1)} %get-tuple-element.10), channel_id=1, source_target_pairs={{0,8},{8,16},{16,24},{24,0},{1,9},{9,17},{17,25},{25,1},{2,10},{10... | collective-permute-start | bytes 884744 | tf_op jit(solution)/shard_map/ppermute | solution.py:18
  160.1 17.5 %collective-permute-start.1 = (bf16[192,768]{1,0:T(8,128)(2,1)}, bf16[192,768]{1,0:T(8,128)(2,1)}, u32[]{:S(2)}, u32[]{:S(2)}) collective-permute-start(bf16[192,768]{1,0:T(8,128)(2,1)} %collective-permute-done), channel_id=1, source_target_pairs={{0,8},{8,16},{16,24},{24,0},{1,9},{9,17},{17,25},{25,1},{2,10},{10... | collective-permute-start | bytes 884744 | tf_op jit(solution)/shard_map/ppermute | solution.py:18
  177.7 14.4 %collective-permute-start.2 = (bf16[192,768]{1,0:T(8,128)(2,1)}, bf16[192,768]{1,0:T(8,128)(2,1)}, u32[]{:S(2)}, u32[]{:S(2)}) collective-permute-start(bf16[192,768]{1,0:T(8,128)(2,1)} %collective-permute-done.1), channel_id=1, source_target_pairs={{0,8},{8,16},{16,24},{24,0},{1,9},{9,17},{17,25},{25,1},{2,10},{10... | collective-permute-start | bytes 884744 | tf_op jit(solution)/shard_map/ppermute | solution.py:18
  226.7 31.9 %all-to-all-start.1 = ((bf16[8,96,1024]{2,1,0:T(8,128)(2,1)}), bf16[8,96,1024]{2,1,0:T(8,128)(2,1)}, u32[]{:S(2)}, u32[]{:S(2)}) async-start(bf16[8,96,1024]{2,1,0:T(8,128)(2,1)} %copy.76), calls=%async_computation.3 | async-start | bytes 3145728 | tf_op jit(solution)/shard_map/all_to_all | solution.py:115
  258.6 4.0 %copy-start.3 = (bf16[8,96,1024]{2,0,1:T(8,128)(2,1)S(1)}, bf16[8,96,1024]{2,0,1:T(8,128)(2,1)}, u32[]{:S(2)}) copy-start(bf16[8,96,1024]{2,0,1:T(8,128)(2,1)} %copy-done.2) | copy-start | bytes 4718596
  258.6 25.0 %all-to-all-start.3 = ((bf16[8,96,1024]{2,1,0:T(8,128)(2,1)}), bf16[8,96,1024]{2,1,0:T(8,128)(2,1)S(1)}, u32[]{:S(2)}, u32[]{:S(2)}) async-start(bf16[8,96,1024]{2,1,0:T(8,128)(2,1)} %copy.84), calls=%async_computation.6 | async-start | bytes 3145728 | tf_op jit(solution)/shard_map/all_to_all | solution.py:122
  262.6 8.1 %copy-start.4 = (s32[1024]{0:T(1024)S(1)}, s32[1024]{0:T(1024)}, u32[]{:S(2)}) copy-start(s32[1024]{0:T(1024)} %pad_clamp_fusion.1) | copy-start | bytes 12292
  283.6 2.1 copy-start.6
  283.6 2.1 copy-start.8
  283.6 4.4 %copy-start.1 = (bf16[48,1024]{1,0:T(8,128)(2,1)S(1)}, bf16[48,1024]{1,0:T(8,128)(2,1)}, u32[]{:S(2)}) copy-start(bf16[48,1024]{1,0:T(8,128)(2,1)} %param.10) | copy-start | bytes 294916
Sparse Core Ops, SparseCore 0:
  55.2 30.7 reduce-scatter.7
  88.9 27.8 reduce-scatter.5
  119.1 27.8 reduce-scatter.3
  149.5 39.1 all-gather.2
  190.2 29.6 all-gather.4
